TPU v7x, 128 devices: a whole 4x4x4 slice. The times are simulated.
128 devices in a mesh: dp: 8 (over z, core), ts: 16 (over y, x).
Axes of the slice: x: 4, y: 4, z: 4, core: 2. Of those that a mesh axis runs over, the one named last changes fastest.
Arguments:
- text_embed: bfloat16 [8, 1024, 4096], P('dp', None, 'ts'), may hold values from -6 to 6
- bridge: bfloat16 [128, 32, 4096], P('dp', None, 'ts'), may hold values from -6 to 6
- crystal_slot: int32 [128], P('dp'), may hold values from 0 to 8159, as said below
- segments: int32 [8, 1024], P('dp'), may hold values from 0 to 15, as said below
- attn_gain: float32 [4096], replicated, may hold values from 0.1 to 1.9
- w_query: bfloat16 [4096, 4096], P(None, 'ts'), as said below
- w_key: bfloat16 [4096, 1024], P(None, 'ts'), may hold values from -0.09375 to 0.09375
- w_value: bfloat16 [4096, 1024], P(None, 'ts'), may hold values from -0.09375 to 0.09375
- w_out: bfloat16 [4096, 4096], P('ts'), may hold values from -0.09375 to 0.09375
- mlp_gain: float32 [4096], replicated, may hold values from 0.1 to 1.9
- w_gate: bfloat16 [4096, 12288], P(None, 'ts'), may hold values from -0.09375 to 0.09375
- w_up: bfloat16 [4096, 12288], P(None, 'ts'), may hold values from -0.09375 to 0.09375
- w_down: bfloat16 [12288, 4096], P('ts'), may hold values from -0.0546875 to 0.0546875
Outputs:
- layer_out: bfloat16 [8, 1024, 4096], P('dp', 'ts')
Inputs may be any that keep to these rules, and one draw needn't show every extreme that they name: `segments`: each row starts at 0, never falls and names every document number of 0 to 15; every document holds at least 33 positions. `crystal_slot`: each crystal's 32 rows take the first 32 positions of one document, given as sequence * 1024 + that document's first position; every document takes exactly one crystal, and each sequence takes exactly 2 of the 16 crystals held by each index of dp. `w_query`: entries lie within plus or minus 104 / sqrt(4096).
All inputs are finite; a program needn't handle non-finite values.
Results may differ from a plain program's by a relative error of at most 0.025.
The roundings to bfloat16 on the way count: a program that leaves them out, or rounds other values in their place, can miss the bound.
Values may be sent and summed in bfloat16 or wider, within the bound.
No kernel may reach another device: no remote copies, remote signals or barrier semaphores. Data moves between devices by JAX's collectives and lax.ppermute only.
A program may use at most 128 MiB of HBM per device.

v0:
```python
import jax
import jax.numpy as jnp
from jax import lax
from jax.sharding import PartitionSpec as P

HD = 128
DOC_LEN = 64
norm_epsilon = 1e-05
rope_base = 500000.0
masked_score = -1e30


def partner_2(block, axis, apart):
    count = lax.axis_size(axis)
    route = []
    for low in range(count):
        high = low | 1 << apart
        if high != low and high < count:
            route += [(low, high), (high, low)]
    return lax.ppermute(block, axis, route)


def norm_rows(rows, gain):
    widened = rows.astype(jnp.float32)
    inverse_rms = lax.rsqrt(jnp.mean(widened * widened, axis=-1, keepdims=True) + norm_epsilon)
    return (widened * inverse_rms * gain).astype(jnp.bfloat16)


def rotate_pairs(values, positions, first_pair):
    pair_count = values.shape[-1] // 2
    exponent = 2.0 * (first_pair + jnp.arange(pair_count, dtype=jnp.int32)).astype(jnp.float32) / HD
    frequency = rope_base ** (-exponent)
    angles = positions.astype(jnp.float32)[:, None] * frequency[None, :]
    cosine = jnp.cos(angles)[:, None, :]
    sine_part = jnp.sin(angles)[:, None, :]
    paired = values.reshape(values.shape[0], values.shape[1], pair_count, 2)
    even_part = paired[..., 0]
    odd_part = paired[..., 1]
    new_even = even_part * cosine - odd_part * sine_part
    new_odd = even_part * sine_part + odd_part * cosine
    return jnp.stack([new_even, new_odd], axis=-1).reshape(values.shape)


def attend_block(query_block, query_segments, query_index, keys_full, values_full, segment_ids):
    scores = jnp.einsum(
        "qhd,kd->hqk", query_block, keys_full, preferred_element_type=jnp.float32
    ) * HD ** (-0.5)
    key_index = jnp.arange(keys_full.shape[0], dtype=jnp.int32)
    allowed = (query_segments[:, None] == segment_ids[None, :]) & (
        key_index[None, :] <= query_index[:, None]
    )
    scores = jnp.where(allowed[None], scores, masked_score)
    row_top = jnp.max(scores, axis=-1, keepdims=True)
    weights = jnp.exp(scores - row_top)
    probabilities = (weights / jnp.sum(weights, axis=-1, keepdims=True)).astype(jnp.bfloat16)
    mixed_rows = jnp.einsum(
        "hqk,kd->qhd", probabilities, values_full, preferred_element_type=jnp.float32
    )
    return mixed_rows.astype(jnp.bfloat16).reshape(query_block.shape[0], -1)


def shards(
    text_embed,
    bridge,
    crystal_slot,
    segments,
    attn_gain,
    w_query,
    w_key,
    w_value,
    w_out,
    mlp_gain,
    w_gate,
    w_up,
    w_down,
):
    seq_len = text_embed.shape[1]
    part_width = text_embed.shape[2]
    doc_count = seq_len // DOC_LEN
    bridge_len = bridge.shape[1]
    tok_rows = seq_len // lax.axis_size("ts")
    group_index = lax.axis_index("dp")
    ts_index = lax.axis_index("ts")
    segment_ids = segments[0]
    doc_numbers = jnp.arange(doc_count, dtype=jnp.int32)
    starts = jnp.sum((segment_ids[None, :] < doc_numbers[:, None]).astype(jnp.int32), axis=1)
    doc_match = segment_ids[:, None] == doc_numbers[None, :]
    positions = jnp.arange(seq_len, dtype=jnp.int32) - jnp.sum(
        jnp.where(doc_match, starts[None, :], 0), axis=1
    )
    flat_bridge = bridge.reshape(bridge.shape[0], bridge_len * part_width)
    arrived, arrived_slots = (
        lax.all_gather(flat_bridge, "dp", axis=0, tiled=True),
        lax.all_gather(crystal_slot, "dp", axis=0, tiled=True),
    )
    wanted = group_index * seq_len + starts
    picking = wanted[:, None] == arrived_slots[None, :]
    by_doc = jnp.dot(
        picking.astype(jnp.bfloat16), arrived, preferred_element_type=jnp.float32
    ).astype(jnp.bfloat16)
    by_doc = by_doc.reshape(doc_count * bridge_len, part_width)
    in_bridge = positions < bridge_len
    row_pick = (segment_ids * bridge_len + positions)[:, None] == jnp.arange(
        doc_count * bridge_len, dtype=jnp.int32
    )[None, :]
    row_pick = row_pick & in_bridge[:, None]
    filled = jnp.dot(
        row_pick.astype(jnp.bfloat16), by_doc, preferred_element_type=jnp.float32
    ).astype(jnp.bfloat16)
    own_part = jnp.where(in_bridge[:, None], filled, text_embed[0])
    packed = lax.all_gather(own_part, "ts", axis=1, tiled=True)
    normed = norm_rows(packed, attn_gain)
    heads_here = w_query.shape[1] // HD
    queries = jnp.dot(normed, w_query, preferred_element_type=jnp.float32).reshape(
        seq_len, heads_here, HD
    )
    queries = rotate_pairs(queries, positions, 0).astype(jnp.bfloat16)
    kv_cols = w_key.shape[1]
    upper_half = ts_index % 2 == 1
    key_half = jnp.dot(normed, w_key, preferred_element_type=jnp.float32).reshape(
        seq_len, 1, kv_cols
    )
    key_half = rotate_pairs(key_half, positions, ts_index % 2 * (kv_cols // 2))
    key_half = key_half.astype(jnp.bfloat16).reshape(seq_len, kv_cols)
    value_half = jnp.dot(normed, w_value, preferred_element_type=jnp.float32).astype(jnp.bfloat16)
    own_pair = jnp.concatenate([key_half, value_half], axis=1)
    partner = partner_2(own_pair, "ts", 0)
    lower_half = jnp.where(upper_half, partner, own_pair)
    higher = jnp.where(upper_half, own_pair, partner)
    keys_full = jnp.concatenate([lower_half[:, :kv_cols], higher[:, :kv_cols]], axis=1)
    values_full = jnp.concatenate([lower_half[:, kv_cols:], higher[:, kv_cols:]], axis=1)
    block_rows = min(512, seq_len)
    outputs = []
    for block_index in range(seq_len // block_rows):
        first_row = block_index * block_rows
        query_index = jnp.arange(first_row, first_row + block_rows, dtype=jnp.int32)
        outputs.append(
            attend_block(
                queries[first_row : first_row + block_rows],
                segment_ids[first_row : first_row + block_rows],
                query_index,
                keys_full,
                values_full,
                segment_ids,
            )
        )
    attended = jnp.concatenate(outputs, axis=0)
    mine_offset = ts_index * tok_rows
    partial_rows = jnp.dot(attended, w_out, preferred_element_type=jnp.float32)
    attn_sum = lax.psum(partial_rows.astype(jnp.bfloat16), "ts").astype(jnp.float32)
    after_all = (packed.astype(jnp.float32) + attn_sum).astype(jnp.bfloat16)
    after_mine = lax.dynamic_slice_in_dim(after_all, mine_offset, tok_rows, 0)
    normed_mlp = norm_rows(after_all, mlp_gain)
    gate_proj = jnp.dot(normed_mlp, w_gate, preferred_element_type=jnp.float32)
    up_proj = jnp.dot(normed_mlp, w_up, preferred_element_type=jnp.float32)
    hidden = (jax.nn.silu(gate_proj) * up_proj).astype(jnp.bfloat16)
    mlp_mine = lax.psum_scatter(
        jnp.dot(hidden, w_down, preferred_element_type=jnp.float32).astype(jnp.bfloat16),
        "ts",
        scatter_dimension=0,
        tiled=True,
    ).astype(jnp.float32)
    layer_rows = (after_mine.astype(jnp.float32) + mlp_mine).astype(jnp.bfloat16)
    return layer_rows.reshape(1, tok_rows, layer_rows.shape[1])


def solution(mesh):
    return jax.shard_map(
        shards,
        mesh=mesh,
        in_specs=(
            P("dp", None, "ts"),
            P("dp", None, "ts"),
            P("dp"),
            P("dp", None),
            P(),
            P(None, "ts"),
            P(None, "ts"),
            P(None, "ts"),
            P("ts", None),
            P(),
            P(None, "ts"),
            P(None, "ts"),
            P("ts", None),
        ),
        out_specs=P("dp", "ts", None),
        check_vma=False,
    )
```

profile of v0, /device:TPU:0, one launch (start us, length us, event | category | flops | bytes accessed | tf_op | source)
XLA Modules:
  0.0 462.7 jit_solution(8637387790045024165)
XLA Ops:
  11.4 10.6 %all-reduce = s32[128]{0:T(128)S(1)} all-reduce(s32[128]{0:T(128)S(1)} %dynamic-update-slice), channel_id=1, replica_groups=mesh['dp'=8,'ts'=16] {'dp'}, use_global_device_ids=true, to_apply=%add | all-reduce | flops 128 | bytes 1024
  24.3 12.6 %all-gather.3.cloned.1.call-done = bf16[128,8192]{1,0:T(8,128)(2,1)} async-done(((bf16[16,8192]{1,0:T(8,128)(2,1)}), bf16[128,8192]{1,0:T(8,128)(2,1)}) %all-gather.3.cloned.1.call-update) | async-done | bytes 2097168 | tf_op jit(solution)/shard_map/all_gather | solution.py:93
  37.0 2.0 convolution_convert_fusion
  39.1 2.7 fusion.36
  42.0 2.3 multiply_cosine_fusion
  45.9 74.7 %all-gather.5.cloned.1.call-done = bf16[1024,4096]{1,0:T(8,128)(2,1)} async-done(((bf16[1024,256]{1,0:T(8,128)(2,1)}), bf16[1024,4096]{1,0:T(8,128)(2,1)}) %all-gather.5.cloned.1.call-update) | async-done | bytes 8388624 | tf_op jit(solution)/shard_map/all_gather | solution.py:111
  120.6 5.1 %fusion.5 = f32[1024]{0:T(1024)S(1)} fusion(bf16[1024,4096]{1,0:T(8,128)(2,1)} %all-gather.5.cloned.1.call-done), kind=kLoop, calls=%fused_computation.10 | loop fusion | flops 12581888 | bytes 8392704 | tf_op jit(solution)/shard_map/reduce_sum | solution.py:25
  125.7 10.4 %fusion.7 = bf16[1024,4096]{1,0:T(8,128)(2,1)} fusion(bf16[1024,4096]{1,0:T(8,128)(2,1)} %all-gather.5.cloned.1.call-done, f32[4096]{0:T(1024)S(1)} %copy-done.8, f32[1024]{0:T(1024)S(1)} %add_rsqrt_fusion.1), kind=kLoop, calls=%fused_computation.12 | loop fusion | flops 16777216 | bytes 16797696 | tf_op jit(solution)/shard_map/convert_element_type | solution.py:26
  136.1 6.2 %convolution_convert_fusion.3 = bf16[1024,64]{0,1:T(8,128)(2,1)S(1)} fusion(bf16[1024,4096]{1,0:T(8,128)(2,1)} %fusion.7, bf16[4096,64]{0,1:T(8,128)(2,1)S(1)} %copy-done.4), kind=kOutput, calls=%fused_computation.48 | convolution fusion | flops 536936448 | bytes 9043968 | tf_op jit(solution)/shard_map/dot_general | solution.py:125
  142.4 2.7 fusion.103
  145.0 3.6 fusion.104
  155.5 2.1 subtract_convert_fusion
  158.9 2.7 collective-permute-done
  161.7 4.8 %fusion.98 = (f32[2,512]{1,0:T(2,128)S(1)}, f32[2,512,1024]{1,2,0:T(8,128)}) fusion(pred[512,1024]{0,1:T(8,128)(4,1)} %get-tuple-element.25, bf16[512,2,128]{0,1,2:T(2,128)(2,1)} %bitcast.86, bf16[1024,64]{0,1:T(8,128)(2,1)S(1)} %get-tuple-element.35, bf16[1024,64]{0,1:T(8,128)(2,1)S(1)} %get-tuple-element.18), kind=kOutput, calls=%fused_computation.119 | convolution fusion | flops 273155072 | bytes 5246976 | tf_op jit(solution)/shard_map/sub | solution.py:54
  166.5 3.7 fusion.93
  170.2 2.8 fusion.40
  174.2 5.6 %convolution_convert_fusion.2 = bf16[1024,4096]{1,0:T(8,128)(2,1)} fusion(bf16[256,4096]{1,0:T(8,128)(2,1)S(1)} %copy-done, bf16[512,256]{0,1:T(8,128)(2,1)S(1)} %bitcast.83, bf16[512,256]{0,1:T(8,128)(2,1)S(1)} %bitcast.82), kind=kOutput, calls=%fused_computation.16 | convolution fusion | flops 2152726528 | bytes 11010048 | tf_op jit(solution)/shard_map/dot_general | solution.py:149
  179.8 140.8 %all-reduce.3.cloned.1.call-done = bf16[1024,4096]{1,0:T(8,128)(2,1)} async-done(((bf16[1024,4096]{1,0:T(8,128)(2,1)}), bf16[1024,4096]{1,0:T(8,128)(2,1)}) %all-reduce.3.cloned.1.call-update) | async-done | bytes 8388624 | tf_op jit(solution)/shard_map/psum | solution.py:150
  320.6 8.0 %fusion.2 = (f32[1024]{0:T(1024)S(1)}, bf16[1024,4096]{1,0:T(8,128)(2,1)S(1)}) fusion(bf16[1024,4096]{1,0:T(8,128)(2,1)} %all-reduce.3.cloned.1.call-done, bf16[1024,4096]{1,0:T(8,128)(2,1)} %all-gather.5.cloned.1.call-done), kind=kLoop, calls=%fused_computation.7 | loop fusion | flops 29359104 | bytes 25169920 | tf_op jit(solution)/shard_map/reduce_sum | solution.py:25
  328.7 3.2 copy-done.3
  331.9 11.3 %fusion.11 = f32[1024,768]{1,0:T(8,128)} fusion(bf16[4096,768]{1,0:T(8,128)(2,1)} %param.24, bf16[1024,4096]{1,0:T(8,128)(2,1)S(1)} %get-tuple-element.6, f32[4096]{0:T(1024)S(1)} %copy-done.10, f32[1024]{0:T(1024)S(1)} %add_rsqrt_fusion), kind=kOutput, calls=%fused_computation.26 | convolution fusion | flops 6459228160 | bytes 17846272 | tf_op jit(solution)/shard_map/dot_general | solution.py:155
  343.2 26.4 %convolution_convert_fusion.1 = bf16[1024,4096]{1,0:T(8,128)(2,1)} fusion(bf16[768,4096]{1,0:T(8,128)(2,1)} %param.25, f32[1024,768]{1,0:T(8,128)} %fusion.11, bf16[4096,768]{1,0:T(8,128)(2,1)} %param.23, bf16[1024,4096]{1,0:T(8,128)(2,1)} %copy-done.3, f32[4096]{0:T(1024)S(1)} %copy-done.10, f32[1024]{0:T(1024)S(1)} %add_rsqrt_fusion), kind=kOutput, calls=%fused_computation.15 | convolution fusion | flops 12910592000 | bytes 32526336 | tf_op jit(solution)/shard_map/dot_general | solution.py:158
  369.6 84.2 %reduce-scatter.2.cloned.1.call-done = bf16[64,4096]{1,0:T(8,128)(2,1)} async-done(((bf16[1024,4096]{1,0:T(8,128)(2,1)}), bf16[64,4096]{1,0:T(8,128)(2,1)}) %reduce-scatter.2.cloned.1.call-update) | async-done | bytes 524304 | tf_op jit(solution)/shard_map/reduce_scatter | solution.py:157
  453.8 2.1 fusion.43
  (62 shorter events, 17.8 us)
Async XLA Ops:
  6.5 167.6 %copy-start = (bf16[256,4096]{1,0:T(8,128)(2,1)S(1)}, bf16[256,4096]{1,0:T(8,128)(2,1)}, u32[]{:S(2)}) copy-start(bf16[256,4096]{1,0:T(8,128)(2,1)} %param.21) | copy-start | bytes 6291460
  6.5 35.4 %copy-start.7 = (s32[1,1024]{1,0:T(1,128)S(1)}, s32[1,1024]{1,0:T(1,128)}, u32[]{:S(2)}) copy-start(s32[1,1024]{1,0:T(1,128)} %param.16) | copy-start | bytes 12292
  6.5 30.4 %all-gather.3.cloned.1.call-start = ((), (), s32[]{:S(2)}) async-start(), calls=%async_computation.1 | async-start | bytes 2359296 | tf_op jit(solution)/shard_map/all_gather | solution.py:93
  8.5 112.1 %all-gather.5.cloned.1.call-start = ((), (), s32[]{:S(2)}) async-start(), calls=%async_computation.2 | async-start | bytes 8912896 | tf_op jit(solution)/shard_map/all_gather | solution.py:111
  39.1 86.6 %copy-start.8 = (f32[4096]{0:T(1024)S(1)}, f32[4096]{0:T(1024)}, u32[]{:S(2)}) copy-start(f32[4096]{0:T(1024)} %param.17) | copy-start | bytes 49156
  41.9 278.8 %all-reduce.3.cloned.1.call-start = ((), (), s32[]{:S(2)}) async-start(), calls=%async_computation.3 | async-start | bytes 16777216 | tf_op jit(solution)/shard_map/psum | solution.py:150
  125.7 10.4 %copy-start.4 = (bf16[4096,64]{0,1:T(8,128)(2,1)S(1)}, bf16[4096,64]{0,1:T(8,128)(2,1)}, u32[]{:S(2)}) copy-start(bf16[4096,64]{0,1:T(8,128)(2,1)} %param.20) | copy-start | bytes 1572868
  136.1 6.2 %copy-start.2 = (bf16[1024,4096]{1,0:T(8,128)(2,1)S(1)}, bf16[1024,4096]{1,0:T(8,128)(2,1)}, u32[]{:S(2)}) copy-start(bf16[1024,4096]{1,0:T(8,128)(2,1)} %fusion.7) | copy-start | bytes 25165828
  136.1 6.2 %copy-start.5 = (bf16[4096,64]{0,1:T(8,128)(2,1)S(1)}, bf16[4096,64]{0,1:T(8,128)(2,1)}, u32[]{:S(2)}) copy-start(bf16[4096,64]{0,1:T(8,128)(2,1)} %param.19) | copy-start | bytes 1572868
  142.3 2.7 copy-start.9
  154.3 7.3 %collective-permute-start = (bf16[1024,128]{0,1:T(8,128)(2,1)S(1)}, bf16[1024,128]{0,1:T(8,128)(2,1)S(1)}, u32[]{:S(2)}, u32[]{:S(2)}) collective-permute-start(bf16[1024,128]{0,1:T(8,128)(2,1)S(1)} %pad_maximum_fusion.1), channel_id=1, source_target_pairs={{0,1},{1,0},{2,3},{3,2},{4,5},{5,4},{6,7},{7,6},{8,9},{9,8},{10,11... | collective-permute-start | bytes 786440 | tf_op jit(solution)/shard_map/ppermute | solution.py:20
  157.6 8.9 %copy-start.6 = (pred[512,1024]{0,1:T(8,128)(4,1)S(1)}, pred[512,1024]{0,1:T(8,128)(4,1)}, u32[]{:S(2)}) copy-start(pred[512,1024]{0,1:T(8,128)(4,1)} %get-tuple-element.26) | copy-start | bytes 1572868
  170.2 3.4 copy-start.11
  179.8 152.1 %copy-start.10 = (f32[4096]{0:T(1024)S(1)}, f32[4096]{0:T(1024)}, u32[]{:S(2)}) copy-start(f32[4096]{0:T(1024)} %param.22) | copy-start | bytes 49156
  179.8 274.0 %reduce-scatter.2.cloned.1.call-start = ((), (), s32[]{:S(2)}) async-start(), calls=%async_computation.4 | async-start | bytes 8912896 | tf_op jit(solution)/shard_map/reduce_scatter | solution.py:157
  328.7 3.2 copy-start.3
  343.2 112.7 %copy-start.1 = (bf16[256,4096]{1,0:T(8,128)(2,1)S(1)}, bf16[256,4096]{1,0:T(8,128)(2,1)}, u32[]{:S(2)}) copy-start(bf16[256,4096]{1,0:T(8,128)(2,1)} %param.21) | copy-start | bytes 6291460
Sparse Core Ops, SparseCore 0:
  9.1 27.8 all-gather.2
  42.0 78.5 all-gather.4
  179.9 140.6 all-reduce.2
  369.7 84.0 reduce-scatter.1
where the time goes:
time: 466 us; the launch traced here: 463 us
  waiting for transfers between devices  315 us (68%)
  matrix products  72.3 us (16%)
  other arithmetic  35.9 us (8%)
  between operations  14.3 us (3%)
  local copies, waits for them, and re-layouts  13.2 us (3%)
  blocking collectives  10.6 us (2%)
    psum x1, waiting for transfers between devices, shards(): lax.psum(partial_rows.astype(jnp.bfloat16), 'ts').astype(jnp.float32)  141 us
    reduce_scatter x1, waiting for transfers between devices, shards(): lax.psum_scatter(jnp.dot(hidden, w_down, preferred_element_type=jnp.float...  84.2 us
    all_gather x1, waiting for transfers between devices, shards(): packed = lax.all_gather(own_part, 'ts', axis=1, tiled=True)  74.7 us
    dot_general x1, matrix products, shards(): jnp.dot(hidden, w_down, preferred_element_type=jnp.float32)  26.4 us
    reduce_sum x2, other arithmetic, norm_rows(): jnp.mean(widened * widened, axis=-1, keepdims=True) + norm_epsilon  13.1 us
    all_gather x1, waiting for transfers between devices, shards(): lax.all_gather(flat_bridge, 'dp', axis=0, tiled=True)  12.6 us
    dot_general x1, matrix products, shards(): up_proj = jnp.dot(normed_mlp, w_up, preferred_element_type=jnp.float32)  11.3 us
    unnamed x1, blocking collectives  10.6 us
  transfers between devices with their start and end apart: 5, of which 5 were waited for; matrix products, arithmetic and copies ran while one was open for 3% of the time, Pallas kernels for 0%

commit v1 on v0

--- a/solution.py
+++ b/solution.py
@@ -108,7 +108,9 @@
         row_pick.astype(jnp.bfloat16), by_doc, preferred_element_type=jnp.float32
     ).astype(jnp.bfloat16)
     own_part = jnp.where(in_bridge[:, None], filled, text_embed[0])
-    packed = lax.all_gather(own_part, "ts", axis=1, tiled=True)
+    packed = jnp.concatenate(
+        lax.all_to_all(jnp.stack([own_part] * lax.axis_size("ts")), "ts", 0, 0), axis=1
+    )
     normed = norm_rows(packed, attn_gain)
     heads_here = w_query.shape[1] // HD
     queries = jnp.dot(normed, w_query, preferred_element_type=jnp.float32).reshape(

time: 466 us -> 558 us (1.20)
  local copies, waits for them, and re-layouts: 13.2 us -> 56.4 us
  waiting for transfers between devices: 315 us -> 353 us
  starting transfers between devices: 1.38 us -> 8.01 us
    all_to_all x0 -> x1, waiting for transfers between devices: none -> 114 us  [shards(): lax.all_to_all(jnp.stack([own_part] * lax.axis_size('ts')), 'ts', 0, 0)]
    all_gather x1 -> x0, waiting for transfers between devices: 74.7 us -> none  [shards(): packed = lax.all_gather(own_part, 'ts', axis=1, tiled=True)]
    convert_element_type x0 -> x1, local copies, waits for them, and re-layouts: none -> 17.5 us  [shards(): after_all = (packed.astype(jnp.float32) + attn_sum).astype(jnp.bfloat16)]
    all_to_all x0 -> x1, local copies, waits for them, and re-layouts: none -> 12.3 us  [shards(): lax.all_to_all(jnp.stack([own_part] * lax.axis_size('ts')), 'ts', 0, 0)]
    dot_general x0 -> x2, local copies, waits for them, and re-layouts: none -> 8.61 us  [shards(): jnp.dot(normed, w_query, preferred_element_type=jnp.float32)]
    all_to_all x0 -> x1, starting transfers between devices: none -> 6.99 us  [shards(): lax.all_to_all(jnp.stack([own_part] * lax.axis_size('ts')), 'ts', 0, 0)]
    unnamed x28 -> x34, local copies, waits for them, and re-layouts: 8.03 us -> 11.2 us
  transfers between devices with their start and end apart: 5 -> 5, of which waited for: 5 -> 5; matrix products, arithmetic and copies ran while one was open for 3% -> 4% of each run, Pallas kernels for 0% -> 0%
where the time goes in v1:
time: 558 us; the launch traced here: 554 us
  waiting for transfers between devices  353 us (63%)
  matrix products  73 us (13%)
  local copies, waits for them, and re-layouts  56.4 us (10%)
  other arithmetic  38.7 us (7%)
  between operations  14.4 us (3%)
  blocking collectives  10.6 us (2%)
  starting transfers between devices  8.01 us (1%)
    psum x1, waiting for transfers between devices, shards(): lax.psum(partial_rows.astype(jnp.bfloat16), 'ts').astype(jnp.float32)  139 us
    all_to_all x1, waiting for transfers between devices, shards(): lax.all_to_all(jnp.stack([own_part] * lax.axis_size('ts')), 'ts', 0, 0)  114 us
    reduce_scatter x1, waiting for transfers between devices, shards(): lax.psum_scatter(jnp.dot(hidden, w_down, preferred_element_type=jnp.float...  84.1 us
    dot_general x1, matrix products, shards(): jnp.dot(hidden, w_down, preferred_element_type=jnp.float32)  26.4 us
    convert_element_type x1, local copies, waits for them, and re-layouts, shards(): after_all = (packed.astype(jnp.float32) + attn_sum).astype(jnp.bfloat16)  17.5 us
    reduce_sum x2, other arithmetic, norm_rows(): jnp.mean(widened * widened, axis=-1, keepdims=True) + norm_epsilon  14.5 us
    all_gather x1, waiting for transfers between devices, shards(): lax.all_gather(flat_bridge, 'dp', axis=0, tiled=True)  12.7 us
    all_to_all x1, local copies, waits for them, and re-layouts, shards(): lax.all_to_all(jnp.stack([own_part] * lax.axis_size('ts')), 'ts', 0, 0)  12.3 us
  transfers between devices with their start and end apart: 5, of which 5 were waited for; matrix products, arithmetic and copies ran while one was open for 4% of the time, Pallas kernels for 0%

profile of v1, /device:TPU:0, one launch (start us, length us, event | category | flops | bytes accessed | tf_op | source)
XLA Modules:
  0.0 553.8 jit_solution(3626922174794946746)
XLA Ops:
  11.4 10.6 %all-reduce = s32[128]{0:T(128)S(1)} all-reduce(s32[128]{0:T(128)S(1)} %dynamic-update-slice), channel_id=1, replica_groups=mesh['dp'=8,'ts'=16] {'dp'}, use_global_device_ids=true, to_apply=%add | all-reduce | flops 128 | bytes 1024
  24.3 12.7 %all-gather.2.cloned.1.call-done = bf16[128,8192]{1,0:T(8,128)(2,1)} async-done(((bf16[16,8192]{1,0:T(8,128)(2,1)}), bf16[128,8192]{1,0:T(8,128)(2,1)}) %all-gather.2.cloned.1.call-update) | async-done | bytes 2097168 | tf_op jit(solution)/shard_map/all_gather | solution.py:93
  41.1 4.0 stack.8
  45.2 7.0 %all-to-all-start = ((bf16[16,1024,256]{2,1,0:T(8,128)(2,1)}), bf16[16,1024,256]{2,1,0:T(8,128)(2,1)}, u32[]{:S(2)}, u32[]{:S(2)}) async-start(bf16[16,1024,256]{2,1,0:T(8,128)(2,1)} %stack.8), calls=%async_computation | async-start | bytes 16777216 | tf_op jit(solution)/shard_map/all_to_all | solution.py:112
  53.1 4.2 copy.66
  57.3 4.4 dot_general.54
  64.4 113.6 %all-to-all-done = bf16[16,1024,256]{2,1,0:T(8,128)(2,1)} async-done(((bf16[16,1024,256]{2,1,0:T(8,128)(2,1)}), bf16[16,1024,256]{2,1,0:T(8,128)(2,1)}, u32[]{:S(2)}, u32[]{:S(2)}) %all-to-all-start) | async-done | bytes 8388640 | tf_op jit(solution)/shard_map/all_to_all | solution.py:112
  178.0 12.3 %copy.61 = bf16[16,1024,256]{1,2,0:T(8,128)(2,1)} copy(bf16[16,1024,256]{2,1,0:T(8,128)(2,1)} %all-to-all-done) | data formatting | bytes 16777216 | tf_op jit(solution)/shard_map/all_to_all | solution.py:112
  190.3 5.1 multiply_reduce_fusion
  195.4 11.3 %convert_element_type.147 = f32[16,1024,256]{1,2,0:T(8,128)} convert(bf16[16,1024,256]{1,2,0:T(8,128)(2,1)} %copy.61) | non-fusion elementwise | flops 4194304 | bytes 25165824 | tf_op jit(solution)/shard_map/convert_element_type | solution.py:153
  206.7 5.0 multiply_convert_fusion.1
  211.7 3.2 copy-done.3
  217.3 17.5 %copy.83 = f32[1024,4096]{1,0:T(8,128)} copy(f32[1024,4096]{0,1:T(8,128)} %bitcast.88) | data formatting | bytes 33554432 | tf_op jit(solution)/shard_map/convert_element_type | solution.py:153
  234.8 8.6 %fusion.42 = bf16[1024,64]{0,1:T(8,128)(2,1)S(1)} fusion(bf16[4096,64]{0,1:T(8,128)(2,1)S(1)} %copy-done.6, f32[1024,4096]{1,0:T(8,128)} %copy.83, f32[4096]{0:T(1024)S(1)} %copy-done.10, f32[1024]{0:T(1024)S(1)} %add_rsqrt_fusion.1), kind=kOutput, calls=%fused_computation.51 | convolution fusion | flops 549519360 | bytes 17453056 | tf_op jit(solution)/shard_map/dot_general | solution.py:127
  248.0 3.1 collective-permute-done
  252.0 4.8 fusion.98
  256.8 4.7 fusion.93
  265.4 5.6 %convolution_convert_fusion.2 = bf16[1024,4096]{1,0:T(8,128)(2,1)} fusion(bf16[256,4096]{1,0:T(8,128)(2,1)S(1)} %copy-done, bf16[512,256]{0,1:T(8,128)(2,1)S(1)} %bitcast.95, bf16[512,256]{0,1:T(8,128)(2,1)S(1)} %bitcast.94), kind=kOutput, calls=%fused_computation.16 | convolution fusion | flops 2152726528 | bytes 11010048 | tf_op jit(solution)/shard_map/dot_general | solution.py:151
  271.3 139.2 %all-reduce.3.cloned.1.call-done = bf16[1024,4096]{1,0:T(8,128)(2,1)} async-done(((bf16[1024,4096]{1,0:T(8,128)(2,1)}), bf16[1024,4096]{1,0:T(8,128)(2,1)}) %all-reduce.3.cloned.1.call-update) | async-done | bytes 8388624 | tf_op jit(solution)/shard_map/psum | solution.py:152
  410.5 9.4 %fusion.2 = (f32[1024]{0:T(1024)S(1)}, bf16[1024,4096]{1,0:T(8,128)(2,1)S(1)}) fusion(f32[1024,4096]{1,0:T(8,128)} %copy.83, bf16[1024,4096]{1,0:T(8,128)(2,1)} %all-reduce.3.cloned.1.call-done), kind=kLoop, calls=%fused_computation.4 | loop fusion | flops 25164800 | bytes 33558528 | tf_op jit(solution)/shard_map/reduce_sum | solution.py:25
  419.9 3.2 copy-done.2
  423.1 11.3 %fusion.10 = f32[1024,768]{1,0:T(8,128)} fusion(bf16[4096,768]{1,0:T(8,128)(2,1)} %param.24, bf16[1024,4096]{1,0:T(8,128)(2,1)S(1)} %get-tuple-element.6, f32[4096]{0:T(1024)S(1)} %copy-done.13, f32[1024]{0:T(1024)S(1)} %add_rsqrt_fusion), kind=kOutput, calls=%fused_computation.26 | convolution fusion | flops 6459228160 | bytes 17846272 | tf_op jit(solution)/shard_map/dot_general | solution.py:157
  434.4 26.4 %convolution_convert_fusion.1 = bf16[1024,4096]{1,0:T(8,128)(2,1)} fusion(bf16[768,4096]{1,0:T(8,128)(2,1)} %param.25, f32[1024,768]{1,0:T(8,128)} %fusion.10, bf16[4096,768]{1,0:T(8,128)(2,1)} %param.23, bf16[1024,4096]{1,0:T(8,128)(2,1)} %copy-done.2, f32[4096]{0:T(1024)S(1)} %copy-done.13, f32[1024]{0:T(1024)S(1)} %add_rsqrt_fusion), kind=kOutput, calls=%fused_computation.15 | convolution fusion | flops 12910592000 | bytes 32526336 | tf_op jit(solution)/shard_map/dot_general | solution.py:160
  460.8 84.1 %reduce-scatter.2.cloned.1.call-done = bf16[64,4096]{1,0:T(8,128)(2,1)} async-done(((bf16[1024,4096]{1,0:T(8,128)(2,1)}), bf16[64,4096]{1,0:T(8,128)(2,1)}) %reduce-scatter.2.cloned.1.call-update) | async-done | bytes 524304 | tf_op jit(solution)/shard_map/reduce_scatter | solution.py:159
  (73 shorter events, 28.2 us)
Async XLA Ops:
  6.5 258.9 %copy-start = (bf16[256,4096]{1,0:T(8,128)(2,1)S(1)}, bf16[256,4096]{1,0:T(8,128)(2,1)}, u32[]{:S(2)}) copy-start(bf16[256,4096]{1,0:T(8,128)(2,1)} %param.21) | copy-start | bytes 6291460
  6.5 30.4 %all-gather.2.cloned.1.call-start = ((), (), s32[]{:S(2)}) async-start(), calls=%async_computation.2 | async-start | bytes 2359296 | tf_op jit(solution)/shard_map/all_gather | solution.py:93
  45.2 7.5 %copy-start.10 = (f32[4096]{0:T(1024)S(1)}, f32[4096]{0:T(1024)}, u32[]{:S(2)}) copy-start(f32[4096]{0:T(1024)} %param.17) | copy-start | bytes 49156
  45.2 7.6 %copy-start.7 = (bf16[4096,64]{0,1:T(8,128)(2,1)S(1)}, bf16[4096,64]{0,1:T(8,128)(2,1)}, u32[]{:S(2)}) copy-start(bf16[4096,64]{0,1:T(8,128)(2,1)} %param.19) | copy-start | bytes 1572868
  45.2 132.8 %all-to-all-start = ((bf16[16,1024,256]{2,1,0:T(8,128)(2,1)}), bf16[16,1024,256]{2,1,0:T(8,128)(2,1)}, u32[]{:S(2)}, u32[]{:S(2)}) async-start(bf16[16,1024,256]{2,1,0:T(8,128)(2,1)} %stack.8), calls=%async_computation | async-start | bytes 16777216 | tf_op jit(solution)/shard_map/all_to_all | solution.py:112
  52.2 9.6 %copy-start.12 = (s32[1,1024]{1,0:T(1,128)S(1)}, s32[1,1024]{1,0:T(1,128)}, u32[]{:S(2)}) copy-start(s32[1,1024]{1,0:T(1,128)} %param.16) | copy-start | bytes 12292
  52.2 358.3 %all-reduce.3.cloned.1.call-start = ((), (), s32[]{:S(2)}) async-start(), calls=%async_computation.3 | async-start | bytes 16777216 | tf_op jit(solution)/shard_map/psum | solution.py:152
  211.7 3.2 copy-start.3
  217.3 17.5 %copy-start.6 = (bf16[4096,64]{0,1:T(8,128)(2,1)S(1)}, bf16[4096,64]{0,1:T(8,128)(2,1)}, u32[]{:S(2)}) copy-start(bf16[4096,64]{0,1:T(8,128)(2,1)} %param.20) | copy-start | bytes 1572868
  234.8 8.9 %copy-start.4 = (bf16[16,1024,256]{1,2,0:T(8,128)(2,1)S(1)}, bf16[16,1024,256]{1,2,0:T(8,128)(2,1)}, u32[]{:S(2)}) copy-start(bf16[16,1024,256]{1,2,0:T(8,128)(2,1)} %copy-done.3) | copy-start | bytes 25165828
  234.8 9.0 %copy-start.5 = (bf16[2,64,2,4096]{3,2,1,0:T(2,128)(2,1)S(1)}, bf16[2,64,2,4096]{3,2,1,0:T(2,128)(2,1)}, u32[]{:S(2)}) copy-start(bf16[2,64,2,4096]{3,2,1,0:T(2,128)(2,1)} %dot_general.54) | copy-start | bytes 6291460
  243.5 7.6 %collective-permute-start = (bf16[1024,128]{0,1:T(8,128)(2,1)S(1)}, bf16[1024,128]{0,1:T(8,128)(2,1)S(1)}, u32[]{:S(2)}, u32[]{:S(2)}) collective-permute-start(bf16[1024,128]{0,1:T(8,128)(2,1)S(1)} %pad_maximum_fusion.1), channel_id=1, source_target_pairs={{0,1},{1,0},{2,3},{3,2},{4,5},{5,4},{6,7},{7,6},{8,9},{9,8},{10,11... | collective-permute-start | bytes 786440 | tf_op jit(solution)/shard_map/ppermute | solution.py:20
  246.5 5.5 copy-start.9
  246.7 10.1 %copy-start.8 = (pred[512,1024]{0,1:T(8,128)(4,1)S(1)}, pred[512,1024]{0,1:T(8,128)(4,1)}, u32[]{:S(2)}) copy-start(pred[512,1024]{0,1:T(8,128)(4,1)} %get-tuple-element.22) | copy-start | bytes 1572868
  256.8 4.7 copy-start.11
  261.5 3.4 copy-start.14
  271.1 152.0 %copy-start.13 = (f32[4096]{0:T(1024)S(1)}, f32[4096]{0:T(1024)}, u32[]{:S(2)}) copy-start(f32[4096]{0:T(1024)} %param.22) | copy-start | bytes 49156
  271.1 273.9 %reduce-scatter.2.cloned.1.call-start = ((), (), s32[]{:S(2)}) async-start(), calls=%async_computation.4 | async-start | bytes 8912896 | tf_op jit(solution)/shard_map/reduce_scatter | solution.py:159
  419.9 3.2 copy-start.2
  434.4 112.7 %copy-start.1 = (bf16[256,4096]{1,0:T(8,128)(2,1)S(1)}, bf16[256,4096]{1,0:T(8,128)(2,1)}, u32[]{:S(2)}) copy-start(bf16[256,4096]{1,0:T(8,128)(2,1)} %param.21) | copy-start | bytes 6291460
Sparse Core Ops, SparseCore 0:
  9.1 27.8 all-gather.1
  271.2 139.2 all-reduce.2
  460.9 83.9 reduce-scatter.1
